TPU v7x, 32 devices: a whole 2x2x4 slice. The times are simulated.
32 devices in a mesh: dp: 4 (over z), tensor: 8 (over y, x, core).
Axes of the slice: x: 2, y: 2, z: 4, core: 2. Of those that a mesh axis runs over, the one named last changes fastest.
Arguments:
- inputs: bfloat16 [4, 32, 4096], P(None, 'tensor', 'dp'), may hold values from -6 to 6
- norm_gain: float32 [4096], P('dp'), may hold values from 0.1 to 1.9
- w_gate: bfloat16 [4096, 28672], P('dp', 'tensor'), may hold values from -0.09375 to 0.09375
- w_up: bfloat16 [4096, 28672], P('dp', 'tensor'), may hold values from -0.09375 to 0.09375
- w_down: bfloat16 [28672, 4096], P('tensor', 'dp'), may hold values from -0.03125 to 0.03125
- d_output: bfloat16 [4, 32, 4096], P(None, 'tensor', 'dp'), may hold values from -0.75 to 0.75
- level_of_batch: int32 [4], replicated, may hold values from 0 to 3, each once
Outputs:
- outputs: bfloat16 [4, 32, 4096], P(None, 'tensor', 'dp')
- d_inputs: bfloat16 [4, 32, 4096], P(None, 'tensor', 'dp')
- d_gain: float32 [4096], P('dp')
- d_gate: bfloat16 [4096, 28672], P('dp', 'tensor')
- d_up: bfloat16 [4096, 28672], P('dp', 'tensor')
- d_down: bfloat16 [28672, 4096], P('tensor', 'dp')
- row_product: float32 [4, 32], P(None, 'tensor')
Inputs may be any that keep to these rules, and one draw needn't show every extreme that they name: `level_of_batch`: every level from 0 to 3 belongs to exactly one micro-batch.
All inputs are finite; a program needn't handle non-finite values.
Results may differ from a plain program's by a relative error of at most 0.02.
Values may be sent and summed in bfloat16 or wider, within the bound.
No kernel may reach another device: no remote copies, remote signals or barrier semaphores. Data moves between devices by JAX's collectives and lax.ppermute only.
A program may use at most 384 MiB of HBM per device.

v0:
```python
import jax
import jax.numpy as jnp
from jax import lax
from jax.sharding import PartitionSpec as P

epsilon = 1e-05
contract_cols = (((1,), (1,)), ((), ()))
contract_rows = (((0,), (0,)), ((), ()))


def local_terms(gate_sum, up_sum, back_sum, active_mask):
    sigmoid_gate = jax.nn.sigmoid(gate_sum)
    silu_gate = gate_sum * sigmoid_gate
    slope = sigmoid_gate * (1.0 + gate_sum * (1.0 - sigmoid_gate))
    hidden = (silu_gate * up_sum * active_mask).astype(jnp.bfloat16)
    gate_grad = (back_sum * up_sum * slope * active_mask).astype(jnp.bfloat16)
    up_grad = (back_sum * silu_gate * active_mask).astype(jnp.bfloat16)
    return (hidden, gate_grad, up_grad)


def per_device(inputs, norm_gain, w_gate, w_up, w_down, d_output, level_of_batch):
    groups = lax.axis_size("tensor")
    tensor_index = lax.axis_index("tensor")
    local_feat = w_gate.shape[0]
    local_cols = w_gate.shape[1]
    full_width = local_feat * lax.axis_size("dp")
    batches, local_rows, _ = inputs.shape
    wide_inputs = inputs.astype(jnp.float32)
    grad_all = lax.all_gather(d_output.transpose(1, 0, 2), "tensor", axis=0, tiled=True)
    rows = grad_all.shape[0]
    start = tensor_index * local_rows
    flat_grad = grad_all.reshape(rows * batches, local_feat)
    back_part = lax.dot_general(
        flat_grad, w_down, contract_cols, preferred_element_type=jnp.float32
    ).astype(jnp.bfloat16)
    back_first = lax.psum(back_part, "dp")
    inputs_all, _ = lax.optimization_barrier((inputs.transpose(1, 0, 2), back_part))
    inputs_all = lax.all_gather(inputs_all, "tensor", axis=0, tiled=True).astype(jnp.float32)
    square_sum = lax.psum(jnp.sum(inputs_all * inputs_all, axis=2).T, "dp").T
    row_scale_all = lax.rsqrt(square_sum / full_width + epsilon)
    normed_all = (inputs_all * row_scale_all[:, :, None] * norm_gain).astype(jnp.bfloat16)
    row_scale = lax.dynamic_slice_in_dim(row_scale_all, start, local_rows, axis=0).T
    flat_normed = normed_all.reshape(rows * batches, local_feat)
    halvings = 3 - level_of_batch
    active = (tensor_index < jnp.right_shift(groups, halvings)).astype(jnp.float32)
    active_mask = jnp.tile(active, rows)[:, None]
    chunks = 1
    width = local_cols // chunks
    down_part = None
    normed_part = None
    hiddens, gate_grads, up_grads = ([], [], [])
    for chunk in range(chunks):
        cols = slice(chunk * width, (chunk + 1) * width)
        gate_w = w_gate[:, cols]
        up_w = w_up[:, cols]
        down_w = w_down[cols, :]
        gate_part = jnp.dot(flat_normed, gate_w, preferred_element_type=jnp.float32)
        up_part = jnp.dot(flat_normed, up_w, preferred_element_type=jnp.float32)
        parts = (gate_part.astype(jnp.bfloat16), up_part.astype(jnp.bfloat16))
        parts, back_sum = lax.optimization_barrier((parts, back_first))
        gate_sum, up_sum = lax.psum(parts, "dp")
        hidden, gate_grad, up_grad = local_terms(
            gate_sum.astype(jnp.float32),
            up_sum.astype(jnp.float32),
            back_sum.astype(jnp.float32),
            active_mask,
        )
        hiddens.append(hidden)
        gate_grads.append(gate_grad)
        up_grads.append(up_grad)
        down_term = jnp.dot(hidden, down_w, preferred_element_type=jnp.float32)
        normed_term = lax.dot_general(
            gate_grad, gate_w, contract_cols, preferred_element_type=jnp.float32
        ) + lax.dot_general(up_grad, up_w, contract_cols, preferred_element_type=jnp.float32)
        down_part = down_term if down_part is None else down_part + down_term
        normed_part = normed_term if normed_part is None else normed_part + normed_term
    hidden = jnp.concatenate(hiddens, axis=1)
    gate_grad = jnp.concatenate(gate_grads, axis=1)
    up_grad = jnp.concatenate(up_grads, axis=1)
    stacked = jnp.stack(
        [
            down_part.reshape(rows, batches, local_feat),
            normed_part.reshape(rows, batches, local_feat),
        ],
        axis=1,
    ).astype(jnp.bfloat16)
    stacked = stacked.reshape(rows, 2 * batches, local_feat)
    scaled_all = (inputs_all * row_scale_all[:, :, None]).reshape(rows * batches, local_feat)
    gain_part = jnp.sum(normed_part * scaled_all, axis=0)
    row_all = jnp.sum(
        normed_part * (norm_gain * inputs_all.reshape(rows * batches, local_feat)), axis=1
    )
    reduced = lax.psum(jnp.concatenate([gain_part, row_all]), "tensor")
    d_gain = reduced[:local_feat]
    row_all = lax.psum(reduced[local_feat:], "dp").reshape(rows, batches)
    row_product = lax.dynamic_slice_in_dim(row_all, start, local_rows, axis=0).T
    hidden, flat_grad, _ = lax.optimization_barrier((hidden, flat_grad, stacked))
    shares = lax.psum_scatter(stacked, "tensor", scatter_dimension=0, tiled=True).astype(
        jnp.float32
    )
    shares = shares.reshape(local_rows, 2, batches, local_feat)
    down_output = shares[:, 0].transpose(1, 0, 2)
    normed_grad = shares[:, 1].transpose(1, 0, 2)
    down_out = lax.dot_general(
        hidden, flat_grad, contract_rows, preferred_element_type=jnp.float32
    ).astype(jnp.bfloat16)
    gate_out = lax.dot_general(
        flat_normed, gate_grad, contract_rows, preferred_element_type=jnp.float32
    ).astype(jnp.bfloat16)
    up_out = lax.dot_general(
        flat_normed, up_grad, contract_rows, preferred_element_type=jnp.float32
    ).astype(jnp.bfloat16)
    wide_grad = d_output.astype(jnp.float32)
    weighted = norm_gain * normed_grad
    outputs = (wide_inputs + down_output).astype(jnp.bfloat16)
    scale_cube = row_scale * row_scale * row_scale
    d_inputs = (
        wide_grad
        + row_scale[:, :, None] * weighted
        - wide_inputs * (scale_cube * row_product / full_width)[:, :, None]
    ).astype(jnp.bfloat16)
    return (outputs, d_inputs, d_gain, gate_out, up_out, down_out, row_product)


def solution(mesh):
    in_specs = (
        P(None, "tensor", "dp"),
        P("dp"),
        P("dp", "tensor"),
        P("dp", "tensor"),
        P("tensor", "dp"),
        P(None, "tensor", "dp"),
        P(),
    )
    out_specs = (
        P(None, "tensor", "dp"),
        P(None, "tensor", "dp"),
        P("dp"),
        P("dp", "tensor"),
        P("dp", "tensor"),
        P("tensor", "dp"),
        P(None, "tensor"),
    )
    return jax.shard_map(
        per_device, mesh=mesh, in_specs=in_specs, out_specs=out_specs, check_vma=False
    )
```

profile of v0, /device:TPU:0, one launch (start us, length us, event | category | flops | bytes accessed | tf_op | source)
XLA Modules:
  0.0 222.1 jit_solution(7097210431955141305)
XLA Ops:
  7.2 0.8 copy.45
  8.0 0.8 copy.44
  8.8 10.8 %all_gather.6 = bf16[32,4,1024]{2,1,0:T(4,128)(2,1)S(1)} all-gather(bf16[4,4,1024]{2,1,0:T(4,128)(2,1)S(1)} %bitcast.61), channel_id=1, replica_groups=mesh['dp'=4,'tensor'=8] {'tensor'}, dimensions={0}, use_global_device_ids=true | all-gather | bytes 294912 | tf_op jit(solution)/shard_map/all_gather | solution.py:29
  19.6 6.6 %convolution_convert_fusion.5 = bf16[128,3584]{1,0:T(8,128)(2,1)} fusion(bf16[128,1024]{1,0:T(8,128)(2,1)S(1)} %reshape.45, bf16[3584,1024]{1,0:T(8,128)(2,1)} %param.11), kind=kOutput, calls=%fused_computation.5 | convolution fusion | flops 939982848 | bytes 8519680 | tf_op jit(solution)/shard_map/dot_general | solution.py:33
  26.4 9.3 %all_gather.7 = bf16[32,4,1024]{2,1,0:T(4,128)(2,1)S(1)} all-gather(bf16[4,4,1024]{2,1,0:T(4,128)(2,1)S(1)} %bitcast.60), channel_id=1, replica_groups=mesh['dp'=4,'tensor'=8] {'tensor'}, dimensions={0}, use_global_device_ids=true | all-gather | bytes 294912 | tf_op jit(solution)/shard_map/all_gather | solution.py:38
  35.7 0.2 multiply_reduce_fusion.2
  36.0 12.4 %psum.42 = f32[4,32]{1,0:T(4,128)S(1)} all-reduce(f32[4,32]{1,0:T(4,128)S(1)} %bitcast.62), channel_id=1, replica_groups=mesh['dp'=4,'tensor'=8] {'dp'}, use_global_device_ids=true, to_apply=%region_1.0 | all-reduce | flops 128 | bytes 1024 | tf_op jit(solution)/shard_map/psum | solution.py:39
  48.5 1.1 broadcast_multiply_fusion
  49.6 1.2 reshape.46
  50.8 5.3 %convolution_convert_fusion.4 = bf16[128,3584]{1,0:T(8,128)(2,1)} fusion(bf16[128,1024]{1,0:T(8,128)(2,1)S(1)} %reshape.46, bf16[1024,3584]{1,0:T(8,128)(2,1)} %param.9), kind=kOutput, calls=%fused_computation.4 | convolution fusion | flops 939982848 | bytes 8519680 | tf_op jit(solution)/shard_map/dot_general | solution.py:57
  56.1 2.1 convolution_convert_fusion.3
  58.2 16.7 %all-reduce.4.cloned.1.call-done = bf16[128,3584]{1,0:T(8,128)(2,1)} async-done(((bf16[128,3584]{1,0:T(8,128)(2,1)}), bf16[128,3584]{1,0:T(8,128)(2,1)}) %all-reduce.4.cloned.1.call-update) | async-done | bytes 917520 | tf_op jit(solution)/shard_map/psum | solution.py:36
  74.9 0.2 reduce-scatter.2.cloned.1.call-start
  75.1 0.8 reshape.50
  75.9 1.0 reshape.49
  77.0 77.6 %all-reduce.6.cloned.1.call-done = (bf16[128,3584]{1,0:T(8,128)(2,1)}, bf16[128,3584]{1,0:T(8,128)(2,1)}) async-done(((bf16[128,3584]{1,0:T(8,128)(2,1)}, bf16[128,3584]{1,0:T(8,128)(2,1)}), (bf16[128,3584]{1,0:T(8,128)(2,1)}, bf16[128,3584]{1,0:T(8,128)(2,1)})) %all-reduce.6.cloned.1.call-update) | async-done | bytes 1835024 | tf_op jit(solution)/shard_map/psum | solution.py:61
  154.6 2.2 %fusion.1 = bf16[128,3584]{1,0:T(8,128)(2,1)S(1)} fusion(bf16[128,3584]{1,0:T(8,128)(2,1)} %get-tuple-element.35, f32[128]{0:T(128)S(1)} %mul.126, bf16[128,3584]{1,0:T(8,128)(2,1)} %get-tuple-element.36), kind=kLoop, calls=%fused_computation.13 | loop fusion | flops 4128768 | bytes 2753024 | tf_op jit(solution)/shard_map/convert_element_type | solution.py:15
  156.9 6.0 %fusion.25 = f32[128,1024]{1,0:T(8,128)S(1)} fusion(bf16[1024,3584]{1,0:T(8,128)(2,1)} %param.9, bf16[128,3584]{1,0:T(8,128)(2,1)S(1)} %copy-done.5, bf16[128,3584]{1,0:T(8,128)(2,1)} %all-reduce.4.cloned.1.call-done, bf16[128,3584]{1,0:T(8,128)(2,1)S(1)} %copy-done.6, f32[128]{0:T(128)S(1)} %mul.126), kind=kOutput, calls=%fused_computation.54 | convolution fusion | flops 945946624 | bytes 10617344 | tf_op jit(solution)/shard_map/dot_general | solution.py:72
  163.0 5.4 %convolution_convert_fusion.1 = bf16[1024,3584]{1,0:T(8,128)(2,1)} fusion(bf16[128,1024]{1,0:T(8,128)(2,1)S(1)} %reshape.46, bf16[128,3584]{1,0:T(8,128)(2,1)S(1)} %copy-done.13, f32[128]{0:T(128)S(1)} %mul.126, bf16[128,3584]{1,0:T(8,128)(2,1)S(1)} %copy-done.6), kind=kOutput, calls=%fused_computation.1 | convolution fusion | flops 947322880 | bytes 9437696 | tf_op jit(solution)/shard_map/dot_general | solution.py:110
  168.4 2.7 %multiply_reduce_fusion.1 = (f32[1024]{0:T(1024)S(1)}, f32[128]{0:T(128)S(1)}, bf16[128,1024]{1,0:T(8,128)(2,1)S(1)}) fusion(f32[128,1024]{1,0:T(8,128)S(1)} %copy-done.9, f32[128,1024]{1,0:T(8,128)S(1)} %copy-done.8, f32[1024]{0:T(1024)S(1)} %copy-done.12, f32[128,1024]{1,0:T(8,128)S(1)} %fusion.25, bf16[1024,3584]{1,0:T(8,128)(2,1)S(1)} %bitcast.57, ...), kind=kOutput, calls=%fused_computation.28 | convolution fusion | flops 944569216 | bytes 11019264 | tf_op jit(solution)/shard_map/dot_general | solution.py:74
  171.0 0.1 stack_reshape.9
  171.2 4.2 %convolution_convert_fusion.6 = bf16[128,1024]{1,0:T(8,128)(2,1)S(1)} fusion(bf16[128,3584]{1,0:T(8,128)(2,1)S(1)} %fusion.1, bf16[3584,1024]{1,0:T(8,128)(2,1)} %param.11), kind=kOutput, calls=%fused_computation.25 | convolution fusion | flops 939655168 | bytes 8519680 | tf_op jit(solution)/shard_map/dot_general | solution.py:71
  175.5 0.1 stack_reshape.8
  175.7 1.1 copy.36
  176.8 5.1 %convolution_convert_fusion = bf16[3584,1024]{1,0:T(8,128)(2,1)} fusion(bf16[128,3584]{1,0:T(8,128)(2,1)S(1)} %fusion.1, bf16[128,1024]{1,0:T(8,128)(2,1)S(1)} %copy-done.3), kind=kOutput, calls=%fused_computation | convolution fusion | flops 943194112 | bytes 8519680 | tf_op jit(solution)/shard_map/dot_general | solution.py:104
  182.0 12.8 %psum.46 = f32[1152]{0:T(1024)S(1)} all-reduce(f32[1152]{0:T(1024)S(1)} %pad_maximum_fusion.1), channel_id=1, replica_groups=mesh['dp'=4,'tensor'=8] {'tensor'}, use_global_device_ids=true, to_apply=%region_8.0 | all-reduce | flops 1152 | bytes 9216 | tf_op jit(solution)/shard_map/psum | solution.py:93
  194.8 0.6 slice.19
  195.6 11.1 %psum.47 = f32[32,4]{0,1:T(4,128)S(1)} all-reduce(f32[32,4]{0,1:T(4,128)S(1)} %copy.39), channel_id=1, replica_groups=mesh['dp'=4,'tensor'=8] {'dp'}, use_global_device_ids=true, to_apply=%region_9.0 | all-reduce | flops 128 | bytes 1024 | tf_op jit(solution)/shard_map/psum | solution.py:95
  206.7 0.7 fusion.20
  207.4 6.6 %convolution_convert_fusion.2 = bf16[1024,3584]{1,0:T(8,128)(2,1)} fusion(bf16[128,1024]{1,0:T(8,128)(2,1)S(1)} %reshape.46, bf16[128,3584]{1,0:T(8,128)(2,1)S(1)} %copy-done.5, bf16[128,3584]{1,0:T(8,128)(2,1)} %all-reduce.4.cloned.1.call-done, bf16[128,3584]{1,0:T(8,128)(2,1)S(1)} %copy-done.7, f32[128]{0:T(128)S(1)} %mul.126), kind=kOutput, calls=%fused_computation.2 | convolution fusion | flops 949616640 | bytes 10355200 | tf_op jit(solution)/shard_map/dot_general | solution.py:107
  214.0 0.9 copy.40
  214.9 0.7 fusion.14
  (60 shorter events, 1.0 us)
Async XLA Ops:
  7.2 67.7 %all-reduce.4.cloned.1.call-start = ((), (), s32[]{:S(2)}) async-start(), calls=%async_computation.1 | async-start | bytes 1835008 | tf_op jit(solution)/shard_map/psum | solution.py:36
  19.6 6.7 %copy-start.2 = (bf16[128,1024]{1,0:T(8,128)(2,1)}, bf16[128,1024]{1,0:T(8,128)(2,1)S(1)}, u32[]{:S(2)}) copy-start(bf16[128,1024]{1,0:T(8,128)(2,1)S(1)} %reshape.45) | copy-start | bytes 786436
  19.6 28.9 %copy-start.12 = (f32[1024]{0:T(1024)S(1)}, f32[1024]{0:T(1024)}, u32[]{:S(2)}) copy-start(f32[1024]{0:T(1024)} %param.8) | copy-start | bytes 12292
  26.3 128.3 %all-reduce.6.cloned.1.call-start = ((), (), s32[]{:S(2)}) async-start(), calls=%async_computation.3 | async-start | bytes 3670016 | tf_op jit(solution)/shard_map/psum | solution.py:61
  35.7 13.9 %copy-start = (bf16[32,4,1024]{2,1,0:T(4,128)(2,1)}, bf16[32,4,1024]{2,1,0:T(4,128)(2,1)S(1)}, u32[]{:S(2)}) copy-start(bf16[32,4,1024]{2,1,0:T(4,128)(2,1)S(1)} %all_gather.7) | copy-start | bytes 786436
  49.6 6.5 %slice-start = ((s8[7340032]{0:T(1024)(128)(4,1)}), s8[3145728]{0:T(1024)(128)(4,1)S(1)}, s32[]{:S(2)}) async-start(s8[7340032]{0:T(1024)(128)(4,1)} %bitcast.54), calls=%async_computation.4 | async-start | bytes 6291456
  50.8 5.3 %slice-start.1 = ((s8[7340032]{0:T(1024)(128)(4,1)}), s8[4194304]{0:T(1024)(128)(4,1)S(1)}, s32[]{:S(2)}) async-start(s8[7340032]{0:T(1024)(128)(4,1)} %bitcast.54), calls=%async_computation.5 | async-start | bytes 8388608
  58.2 17.0 %copy-start.1 = (bf16[32,4,1024]{2,1,0:T(4,128)(2,1)S(1)}, bf16[32,4,1024]{2,1,0:T(4,128)(2,1)}, u32[]{:S(2)}) copy-start(bf16[32,4,1024]{2,1,0:T(4,128)(2,1)} %copy-done) | copy-start | bytes 786436
  58.2 17.8 %copy-start.4 = (f32[32,4,1024]{2,1,0:T(4,128)S(1)}, f32[32,4,1024]{2,1,0:T(4,128)}, u32[]{:S(2)}) copy-start(f32[32,4,1024]{2,1,0:T(4,128)} %get-tuple-element.41) | copy-start | bytes 1572868
  58.2 18.8 %copy-start.14 = (s32[4]{0:T(128)S(1)}, s32[4]{0:T(128)}, u32[]{:S(2)}) copy-start(s32[4]{0:T(128)} %param.13) | copy-start | bytes 52
  74.9 139.1 %reduce-scatter.2.cloned.1.call-start = ((), (), s32[]{:S(2)}) async-start(), calls=%async_computation.2 | async-start | bytes 589824 | tf_op jit(solution)/shard_map/reduce_scatter | solution.py:98
  154.6 2.3 %copy-start.5 = (bf16[128,3584]{1,0:T(8,128)(2,1)S(1)}, bf16[128,3584]{1,0:T(8,128)(2,1)}, u32[]{:S(2)}) copy-start(bf16[128,3584]{1,0:T(8,128)(2,1)} %get-tuple-element.35) | copy-start | bytes 2752516
  154.6 2.3 %copy-start.6 = (bf16[128,3584]{1,0:T(8,128)(2,1)S(1)}, bf16[128,3584]{1,0:T(8,128)(2,1)}, u32[]{:S(2)}) copy-start(bf16[128,3584]{1,0:T(8,128)(2,1)} %get-tuple-element.36) | copy-start | bytes 2752516
  154.6 13.7 %slice-start.2 = ((s8[7340032]{0:T(1024)(128)(4,1)}), s8[4194304]{0:T(1024)(128)(4,1)S(1)}, s32[]{:S(2)}) async-start(s8[7340032]{0:T(1024)(128)(4,1)} %bitcast.56), calls=%async_computation.6 | async-start | bytes 8388608
  156.9 6.1 %copy-start.13 = (bf16[128,3584]{1,0:T(8,128)(2,1)S(1)}, bf16[128,3584]{1,0:T(8,128)(2,1)}, u32[]{:S(2)}) copy-start(bf16[128,3584]{1,0:T(8,128)(2,1)} %all-reduce.4.cloned.1.call-done) | copy-start | bytes 2752516
  156.9 11.5 %slice-start.3 = ((s8[7340032]{0:T(1024)(128)(4,1)}), s8[3145728]{0:T(1024)(128)(4,1)S(1)}, s32[]{:S(2)}) async-start(s8[7340032]{0:T(1024)(128)(4,1)} %bitcast.56), calls=%async_computation.7 | async-start | bytes 6291456
  162.9 5.4 %copy-start.8 = (f32[128,1024]{1,0:T(8,128)S(1)}, f32[128,1024]{1,0:T(8,128)}, u32[]{:S(2)}) copy-start(f32[128,1024]{1,0:T(8,128)} %reshape.50) | copy-start | bytes 1572868
  163.0 5.4 %copy-start.9 = (f32[128,1024]{1,0:T(8,128)S(1)}, f32[128,1024]{1,0:T(8,128)}, u32[]{:S(2)}) copy-start(f32[128,1024]{1,0:T(8,128)} %reshape.49) | copy-start | bytes 1572868
  175.5 1.4 copy-start.3
  176.8 30.5 %copy-start.7 = (bf16[128,3584]{1,0:T(8,128)(2,1)S(1)}, bf16[128,3584]{1,0:T(8,128)(2,1)}, u32[]{:S(2)}) copy-start(bf16[128,3584]{1,0:T(8,128)(2,1)} %get-tuple-element.36) | copy-start | bytes 2752516
  207.4 7.5 %copy-start.10 = (bf16[4,4,1024]{2,1,0:T(4,128)(2,1)S(1)}, bf16[4,4,1024]{2,1,0:T(4,128)(2,1)}, u32[]{:S(2)}) copy-start(bf16[4,4,1024]{2,1,0:T(4,128)(2,1)} %param.7) | copy-start | bytes 98308
  207.4 7.5 %copy-start.11 = (bf16[4,4,1024]{2,1,0:T(4,128)(2,1)S(1)}, bf16[4,4,1024]{2,1,0:T(4,128)(2,1)}, u32[]{:S(2)}) copy-start(bf16[4,4,1024]{2,1,0:T(4,128)(2,1)} %param.12) | copy-start | bytes 98308
Sparse Core Ops, SparseCore 0:
  26.4 48.3 all-reduce.3
  77.8 76.7 all-reduce.5
  176.9 33.0 reduce-scatter.1
where the time goes:
time: 223 us; the launch traced here: 222 us
  waiting for transfers between devices  94.3 us (42%)
  blocking collectives  56.5 us (25%)
  matrix products  44 us (20%)
  between operations  14 us (6%)
  local copies, waits for them, and re-layouts  8.07 us (4%)
  other arithmetic  4.98 us (2%)
    psum x1, waiting for transfers between devices, per_device(): gate_sum, up_sum = lax.psum(parts, 'dp')  77.6 us
    psum x1, waiting for transfers between devices, per_device(): back_first = lax.psum(back_part, 'dp')  16.7 us
    psum x1, blocking collectives, per_device(): reduced = lax.psum(jnp.concatenate([gain_part, row_all]), 'tensor')  12.8 us
    psum x1, blocking collectives, per_device(): square_sum = lax.psum(jnp.sum(inputs_all * inputs_all, axis=2).T, 'dp').T  12.4 us
    psum x1, blocking collectives, per_device(): row_all = lax.psum(reduced[local_feat:], 'dp').reshape(rows, batches)  11.1 us
    all_gather x1, blocking collectives, per_device(): lax.all_gather(d_output.transpose(1, 0, 2), 'tensor', axis=0, tiled=True)  10.8 us
    all_gather x1, blocking collectives, per_device(): lax.all_gather(inputs_all, 'tensor', axis=0, tiled=True).astype(jnp.float32)  9.28 us
    dot_general x1, matrix products, per_device(): lax.dot_general(flat_grad, w_down, contract_cols, preferred_element_type=...  6.65 us
  transfers between devices with their start and end apart: 3, of which 2 were waited for; matrix products, arithmetic and copies ran while one was open for 11% of the time, Pallas kernels for 0%

commit v1 on v0

--- a/solution.py
+++ b/solution.py
@@ -6,6 +6,15 @@
 epsilon = 1e-05
 contract_cols = (((1,), (1,)), ((), ()))
 contract_rows = (((0,), (0,)), ((), ()))
+
+
+def doubling_sum(x, mesh_axis):
+    n_dev = lax.axis_size(mesh_axis)
+    acc, hop = (x, 1)
+    while hop < n_dev:
+        acc = acc + lax.ppermute(acc, mesh_axis, [(i, i ^ hop) for i in range(n_dev)])
+        hop = 2 * hop
+    return acc
 
 
 def local_terms(gate_sum, up_sum, back_sum, active_mask):
@@ -33,7 +42,7 @@
     back_part = lax.dot_general(
         flat_grad, w_down, contract_cols, preferred_element_type=jnp.float32
     ).astype(jnp.bfloat16)
-    back_first = lax.psum(back_part, "dp")
+    back_first = doubling_sum(back_part, "dp")
     inputs_all, _ = lax.optimization_barrier((inputs.transpose(1, 0, 2), back_part))
     inputs_all = lax.all_gather(inputs_all, "tensor", axis=0, tiled=True).astype(jnp.float32)
     square_sum = lax.psum(jnp.sum(inputs_all * inputs_all, axis=2).T, "dp").T

time: 223 us -> 242 us (1.085)
  waiting for transfers between devices: 94.3 us -> 108 us
  blocking collectives: 56.5 us -> 60.9 us
    ppermute x0 -> x2, waiting for transfers between devices: none -> 33.5 us  [doubling_sum(): lax.ppermute(acc, mesh_axis, [(i, i ^ hop) for i in range(n_dev)])]
    psum x1 -> x0, waiting for transfers between devices: 16.7 us -> none  [per_device(): back_first = lax.psum(back_part, 'dp')]
    psum x1, blocking collectives: 12.4 us -> 16.9 us  [per_device(): square_sum = lax.psum(jnp.sum(inputs_all * inputs_all, axis=2).T, 'dp').T]
    psum x1, waiting for transfers between devices: 77.6 us -> 74.8 us  [per_device(): gate_sum, up_sum = lax.psum(parts, 'dp')]
    add x0 -> x2, other arithmetic: none -> 2.69 us  [doubling_sum(): acc + lax.ppermute(acc, mesh_axis, [(i, i ^ hop) for i in range(n_dev)])]
  transfers between devices with their start and end apart: 3 -> 4, of which waited for: 2 -> 2; matrix products, arithmetic and copies ran while one was open for 11% -> 9% of each run, Pallas kernels for 0% -> 0%
where the time goes in v1:
time: 242 us; the launch traced here: 241 us
  waiting for transfers between devices  108 us (45%)
  blocking collectives  60.9 us (25%)
  matrix products  43.4 us (18%)
  between operations  14.3 us (6%)
  other arithmetic  6.79 us (3%)
  local copies, waits for them, and re-layouts  5.72 us (2%)
    psum x1, waiting for transfers between devices, per_device(): gate_sum, up_sum = lax.psum(parts, 'dp')  74.8 us
    ppermute x2, waiting for transfers between devices, doubling_sum(): lax.ppermute(acc, mesh_axis, [(i, i ^ hop) for i in range(n_dev)])  33.5 us
    psum x1, blocking collectives, per_device(): square_sum = lax.psum(jnp.sum(inputs_all * inputs_all, axis=2).T, 'dp').T  16.9 us
    psum x1, blocking collectives, per_device(): reduced = lax.psum(jnp.concatenate([gain_part, row_all]), 'tensor')  12.8 us
    psum x1, blocking collectives, per_device(): row_all = lax.psum(reduced[local_feat:], 'dp').reshape(rows, batches)  11.2 us
    all_gather x1, blocking collectives, per_device(): lax.all_gather(d_output.transpose(1, 0, 2), 'tensor', axis=0, tiled=True)  10.8 us
    all_gather x1, blocking collectives, per_device(): lax.all_gather(inputs_all, 'tensor', axis=0, tiled=True).astype(jnp.float32)  9.28 us
    dot_general x1, matrix products, per_device(): lax.dot_general(flat_normed, gate_grad, contract_rows, preferred_element_...  6.6 us
  transfers between devices with their start and end apart: 4, of which 2 were waited for; matrix products, arithmetic and copies ran while one was open for 9% of the time, Pallas kernels for 0%

profile of v1, /device:TPU:0, one launch (start us, length us, event | category | flops | bytes accessed | tf_op | source)
XLA Modules:
  0.0 241.4 jit_solution(16646918865670711454)
XLA Ops:
  7.2 0.8 copy.44
  8.0 10.8 %all_gather.6 = bf16[32,4,1024]{2,1,0:T(4,128)(2,1)S(1)} all-gather(bf16[4,4,1024]{2,1,0:T(4,128)(2,1)S(1)} %bitcast.60), channel_id=1, replica_groups=mesh['dp'=4,'tensor'=8] {'tensor'}, dimensions={0}, use_global_device_ids=true | all-gather | bytes 294912 | tf_op jit(solution)/shard_map/all_gather | solution.py:38
  18.9 5.6 %convolution_convert_fusion.5 = bf16[128,3584]{1,0:T(8,128)(2,1)S(1)} fusion(bf16[128,1024]{1,0:T(8,128)(2,1)S(1)} %reshape.45, bf16[3584,1024]{1,0:T(8,128)(2,1)} %param.11), kind=kOutput, calls=%fused_computation.5 | convolution fusion | flops 939982848 | bytes 8519680 | tf_op jit(solution)/shard_map/dot_general | solution.py:42
  24.5 1.6 collective-permute-start
  26.2 9.3 %all_gather.7 = bf16[32,4,1024]{2,1,0:T(4,128)(2,1)S(1)} all-gather(bf16[4,4,1024]{2,1,0:T(4,128)(2,1)S(1)} %bitcast.61), channel_id=1, replica_groups=mesh['dp'=4,'tensor'=8] {'tensor'}, dimensions={0}, use_global_device_ids=true | all-gather | bytes 294912 | tf_op jit(solution)/shard_map/all_gather | solution.py:47
  35.4 0.2 multiply_reduce_fusion.2
  35.7 16.9 %psum.35 = f32[4,32]{1,0:T(4,128)S(1)} all-reduce(f32[4,32]{1,0:T(4,128)S(1)} %bitcast.62), channel_id=1, replica_groups=mesh['dp'=4,'tensor'=8] {'dp'}, use_global_device_ids=true, to_apply=%region_1.0 | all-reduce | flops 128 | bytes 1024 | tf_op jit(solution)/shard_map/psum | solution.py:48
  52.7 0.2 broadcast_multiply_fusion
  53.0 1.5 add.46
  54.7 5.3 %convolution_convert_fusion.4 = bf16[128,3584]{1,0:T(8,128)(2,1)} fusion(bf16[128,1024]{1,0:T(8,128)(2,1)S(1)} %reshape.46, bf16[1024,3584]{1,0:T(8,128)(2,1)} %param.9), kind=kOutput, calls=%fused_computation.4 | convolution fusion | flops 939982848 | bytes 8519680 | tf_op jit(solution)/shard_map/dot_general | solution.py:66
  60.0 2.1 convolution_convert_fusion.3
  62.0 33.5 %collective-permute-done.1 = bf16[128,3584]{1,0:T(8,128)(2,1)S(1)} collective-permute-done((bf16[128,3584]{1,0:T(8,128)(2,1)S(1)}, bf16[128,3584]{1,0:T(8,128)(2,1)S(1)}, u32[]{:S(2)}, u32[]{:S(2)}) %collective-permute-start.1) | collective-permute-done | bytes 917536 | tf_op jit(solution)/shard_map/ppermute | solution.py:15
  95.5 1.2 add.47
  96.7 0.2 reduce-scatter.2.cloned.1.call-start
  97.0 0.2 reshape.49
  97.2 0.1 copy-done.8
  97.4 74.8 %all-reduce.3.cloned.1.call-done = (bf16[128,3584]{1,0:T(8,128)(2,1)}, bf16[128,3584]{1,0:T(8,128)(2,1)}) async-done(((bf16[128,3584]{1,0:T(8,128)(2,1)}, bf16[128,3584]{1,0:T(8,128)(2,1)}), (bf16[128,3584]{1,0:T(8,128)(2,1)}, bf16[128,3584]{1,0:T(8,128)(2,1)})) %all-reduce.3.cloned.1.call-update) | async-done | bytes 1835024 | tf_op jit(solution)/shard_map/psum | solution.py:70
  172.2 2.2 fusion.1
  174.5 5.8 %fusion.25 = f32[128,1024]{1,0:T(8,128)S(1)} fusion(bf16[1024,3584]{1,0:T(8,128)(2,1)} %param.9, bf16[128,3584]{1,0:T(8,128)(2,1)S(1)} %copy-done, bf16[128,3584]{1,0:T(8,128)(2,1)S(1)} %copy-done.4, bf16[128,3584]{1,0:T(8,128)(2,1)S(1)} %copy-done.2, f32[128]{0:T(128)S(1)} %mul.126), kind=kOutput, calls=%fused_computation.54 | convolution fusion | flops 945946624 | bytes 10617344 | tf_op jit(solution)/shard_map/dot_general | solution.py:81
  180.3 5.4 %convolution_convert_fusion.1 = bf16[1024,3584]{1,0:T(8,128)(2,1)} fusion(bf16[128,1024]{1,0:T(8,128)(2,1)S(1)} %reshape.46, bf16[128,3584]{1,0:T(8,128)(2,1)S(1)} %copy-done.4, f32[128]{0:T(128)S(1)} %mul.126, bf16[128,3584]{1,0:T(8,128)(2,1)S(1)} %copy-done.2), kind=kOutput, calls=%fused_computation.1 | convolution fusion | flops 947322880 | bytes 9437696 | tf_op jit(solution)/shard_map/dot_general | solution.py:119
  185.7 3.3 %multiply_reduce_fusion.1 = (f32[1024]{0:T(1024)S(1)}, f32[128]{0:T(128)S(1)}, bf16[128,1024]{1,0:T(8,128)(2,1)}) fusion(f32[128,1024]{1,0:T(8,128)S(1)} %reshape.49, f32[128,1024]{1,0:T(8,128)S(1)} %reshape.50, f32[1024]{0:T(1024)S(1)} %copy-done.7, f32[128,1024]{1,0:T(8,128)S(1)} %fusion.25, bf16[1024,3584]{1,0:T(8,128)(2,1)S(1)} %bitcast.57, ...), kind=kOutput, calls=%fused_computation.28 | convolution fusion | flops 944569216 | bytes 11019264 | tf_op jit(solution)/shard_map/dot_general | solution.py:83
  189.0 1.1 stack_reshape.9
  190.1 4.2 %convolution_convert_fusion.6 = bf16[128,1024]{1,0:T(8,128)(2,1)S(1)} fusion(bf16[128,3584]{1,0:T(8,128)(2,1)S(1)} %fusion.1, bf16[3584,1024]{1,0:T(8,128)(2,1)} %param.11), kind=kOutput, calls=%fused_computation.25 | convolution fusion | flops 939655168 | bytes 8519680 | tf_op jit(solution)/shard_map/dot_general | solution.py:80
  194.6 1.1 copy.36
  195.7 5.1 %convolution_convert_fusion = bf16[3584,1024]{1,0:T(8,128)(2,1)} fusion(bf16[128,3584]{1,0:T(8,128)(2,1)S(1)} %fusion.1, bf16[128,1024]{1,0:T(8,128)(2,1)S(1)} %reshape.45), kind=kOutput, calls=%fused_computation | convolution fusion | flops 943194112 | bytes 8519680 | tf_op jit(solution)/shard_map/dot_general | solution.py:113
  200.9 12.8 %psum.38 = f32[1152]{0:T(1024)S(1)} all-reduce(f32[1152]{0:T(1024)S(1)} %pad_maximum_fusion.1), channel_id=1, replica_groups=mesh['dp'=4,'tensor'=8] {'tensor'}, use_global_device_ids=true, to_apply=%region_7.0 | all-reduce | flops 1152 | bytes 9216 | tf_op jit(solution)/shard_map/psum | solution.py:102
  213.7 0.6 slice.19
  214.5 11.2 %psum.39 = f32[32,4]{0,1:T(4,128)S(1)} all-reduce(f32[32,4]{0,1:T(4,128)S(1)} %copy.39), channel_id=1, replica_groups=mesh['dp'=4,'tensor'=8] {'dp'}, use_global_device_ids=true, to_apply=%region_8.0 | all-reduce | flops 128 | bytes 1024 | tf_op jit(solution)/shard_map/psum | solution.py:104
  225.7 0.7 fusion.20
  226.3 6.6 %convolution_convert_fusion.2 = bf16[1024,3584]{1,0:T(8,128)(2,1)} fusion(bf16[128,1024]{1,0:T(8,128)(2,1)S(1)} %reshape.46, bf16[128,3584]{1,0:T(8,128)(2,1)S(1)} %copy-done.1, bf16[128,3584]{1,0:T(8,128)(2,1)} %add.47, bf16[128,3584]{1,0:T(8,128)(2,1)S(1)} %copy-done.3, f32[128]{0:T(128)S(1)} %mul.126), kind=kOutput, calls=%fused_computation.2 | convolution fusion | flops 949616640 | bytes 10355200 | tf_op jit(solution)/shard_map/dot_general | solution.py:116
  232.9 0.9 copy.40
  233.8 0.7 fusion.14
  (51 shorter events, 1.2 us)
Async XLA Ops:
  7.2 165.1 %all-reduce.3.cloned.1.call-start = ((), (), s32[]{:S(2)}) async-start(), calls=%async_computation.2 | async-start | bytes 3670016 | tf_op jit(solution)/shard_map/psum | solution.py:70
  18.8 7.3 %copy-start.5 = (bf16[4,4,1024]{2,1,0:T(4,128)(2,1)S(1)}, bf16[4,4,1024]{2,1,0:T(4,128)(2,1)}, u32[]{:S(2)}) copy-start(bf16[4,4,1024]{2,1,0:T(4,128)(2,1)} %param.7) | copy-start | bytes 98308
  18.9 33.8 %copy-start.7 = (f32[1024]{0:T(1024)S(1)}, f32[1024]{0:T(1024)}, u32[]{:S(2)}) copy-start(f32[1024]{0:T(1024)} %param.8) | copy-start | bytes 12292
  24.5 28.5 %collective-permute-start = (bf16[128,3584]{1,0:T(8,128)(2,1)S(1)}, bf16[128,3584]{1,0:T(8,128)(2,1)}, u32[]{:S(2)}, u32[]{:S(2)}) collective-permute-start(bf16[128,3584]{1,0:T(8,128)(2,1)S(1)} %convolution_convert_fusion.5), channel_id=1, source_target_pairs={{0,8},{8,0},{16,24},{24,16},{1,9},{9,1},{17,25},{25,17},{2,10},{10... | collective-permute-start | bytes 2752520 | tf_op jit(solution)/shard_map/ppermute | solution.py:15
  53.0 6.9 %slice-start = ((s8[7340032]{0:T(1024)(128)(4,1)}), s8[4194304]{0:T(1024)(128)(4,1)S(1)}, s32[]{:S(2)}) async-start(s8[7340032]{0:T(1024)(128)(4,1)} %bitcast.54), calls=%async_computation.3 | async-start | bytes 8388608
  54.6 5.4 %slice-start.1 = ((s8[7340032]{0:T(1024)(128)(4,1)}), s8[3145728]{0:T(1024)(128)(4,1)S(1)}, s32[]{:S(2)}) async-start(s8[7340032]{0:T(1024)(128)(4,1)} %bitcast.54), calls=%async_computation.4 | async-start | bytes 6291456
  54.6 40.9 %collective-permute-start.1 = (bf16[128,3584]{1,0:T(8,128)(2,1)S(1)}, bf16[128,3584]{1,0:T(8,128)(2,1)S(1)}, u32[]{:S(2)}, u32[]{:S(2)}) collective-permute-start(bf16[128,3584]{1,0:T(8,128)(2,1)S(1)} %add.46), channel_id=1, source_target_pairs={{0,16},{8,24},{16,0},{24,8},{1,17},{9,25},{17,1},{25,9},{2,18},{10... | collective-permute-start | bytes 2752520 | tf_op jit(solution)/shard_map/ppermute | solution.py:15
  96.7 0.7 copy-start.8
  96.7 136.2 %reduce-scatter.2.cloned.1.call-start = ((), (), s32[]{:S(2)}) async-start(), calls=%async_computation.1 | async-start | bytes 589824 | tf_op jit(solution)/shard_map/reduce_scatter | solution.py:107
  97.0 77.5 %copy-start.4 = (bf16[128,3584]{1,0:T(8,128)(2,1)S(1)}, bf16[128,3584]{1,0:T(8,128)(2,1)}, u32[]{:S(2)}) copy-start(bf16[128,3584]{1,0:T(8,128)(2,1)} %add.47) | copy-start | bytes 2752516
  172.2 2.3 copy-start
  172.2 2.3 copy-start.2
  172.2 13.5 %slice-start.2 = ((s8[7340032]{0:T(1024)(128)(4,1)}), s8[4194304]{0:T(1024)(128)(4,1)S(1)}, s32[]{:S(2)}) async-start(s8[7340032]{0:T(1024)(128)(4,1)} %bitcast.56), calls=%async_computation.5 | async-start | bytes 8388608
  174.5 11.2 %slice-start.3 = ((s8[7340032]{0:T(1024)(128)(4,1)}), s8[3145728]{0:T(1024)(128)(4,1)S(1)}, s32[]{:S(2)}) async-start(s8[7340032]{0:T(1024)(128)(4,1)} %bitcast.56), calls=%async_computation.6 | async-start | bytes 6291456
  195.7 30.6 %copy-start.1 = (bf16[128,3584]{1,0:T(8,128)(2,1)S(1)}, bf16[128,3584]{1,0:T(8,128)(2,1)}, u32[]{:S(2)}) copy-start(bf16[128,3584]{1,0:T(8,128)(2,1)} %get-tuple-element.35) | copy-start | bytes 2752516
  195.7 30.6 %copy-start.3 = (bf16[128,3584]{1,0:T(8,128)(2,1)S(1)}, bf16[128,3584]{1,0:T(8,128)(2,1)}, u32[]{:S(2)}) copy-start(bf16[128,3584]{1,0:T(8,128)(2,1)} %get-tuple-element.36) | copy-start | bytes 2752516
  226.3 7.5 %copy-start.6 = (bf16[4,4,1024]{2,1,0:T(4,128)(2,1)S(1)}, bf16[4,4,1024]{2,1,0:T(4,128)(2,1)}, u32[]{:S(2)}) copy-start(bf16[4,4,1024]{2,1,0:T(4,128)(2,1)} %param.12) | copy-start | bytes 98308
Sparse Core Ops, SparseCore 0:
  96.8 75.3 all-reduce.2
  195.8 33.1 reduce-scatter.1
